TPU v7x, 256 devices: a whole 4x4x8 slice. The times are simulated.
256 devices in a mesh: dp: 32 (over x, z), own: 8 (over y, core).
Axes of the slice: x: 4, y: 4, z: 8, core: 2. Of those that a mesh axis runs over, the one named last changes fastest.
Arguments:
- partials: bfloat16 [32, 64, 256, 1024], P('dp', None, None, 'own')
- owner: int32 [64, 1], replicated, may hold values from 0 to 31; in each aligned block of 64 rows (0 to 63, 64 to 127, ...) at most 4 rows name the same one
- momentum: float32 [32, 4, 256, 1024], P('dp', None, None, 'own'), may hold values from -1.2 to 1.2
- master: float32 [32, 4, 256, 1024], P('dp', None, None, 'own'), may hold values from -0.3 to 0.3
Outputs:
- new_momentum: float32 [32, 4, 256, 1024], P('dp', None, None, 'own')
- new_master: float32 [32, 4, 256, 1024], P('dp', None, None, 'own')
- new_weights: bfloat16 [64, 256, 1024], P(None, None, 'own')
Inputs may be any that keep to these rules, and one draw needn't show every extreme that they name: `owner`: every group owns at least one block and at most 4 blocks; some group owns exactly 4.
All inputs are finite; a program needn't handle non-finite values.
Results may differ from a plain program's by a relative error of at most 0.0007.
Values may be sent and summed in bfloat16 or wider, within the bound.
No kernel may reach another device: no remote copies, remote signals or barrier semaphores. Data moves between devices by JAX's collectives and lax.ppermute only.
A program may use at most 128 MiB of HBM per device.

v0:
```python
import math
import jax
import jax.numpy as jnp
from jax import lax
from jax.sharding import PartitionSpec as P

D = 1024
ITERS = 5
COEF_A = 3.4445
COEF_B = -4.775
COEF_C = 2.0315
BETA = 0.95
STEP_SIZE = 0.2
DECAY = 0.1
EPSILON = 1e-07


def slot_targets(owner_list, group_count, slot_count):
    onehot = (owner_list[:, None] == jnp.arange(group_count, dtype=jnp.int32)[None, :]).astype(
        jnp.int32
    )
    before = jnp.cumsum(onehot, axis=0) - onehot
    ranks = jnp.sum(before * onehot, axis=1)
    return owner_list * slot_count + ranks


def slot_sources(target, slot_count, block_count):
    positions = jnp.arange(slot_count, dtype=jnp.int32)
    matches = positions[:, None] == target[None, :]
    present = jnp.any(matches, axis=1)
    source = jnp.sum(
        jnp.where(matches, jnp.arange(block_count, dtype=jnp.int32)[None, :], 0), axis=1
    )
    return (present, source)


def local_gram(values):
    return jnp.einsum(
        "srk,stk->srt",
        values,
        values,
        precision=lax.Precision.HIGHEST,
        preferred_element_type=jnp.float32,
    )


def gram_total(values):
    return lax.psum(local_gram(values), "own")


def newton_turn(ortho, gram):
    square = jnp.einsum(
        "srt,stu->sru",
        gram,
        gram,
        precision=lax.Precision.HIGHEST,
        preferred_element_type=jnp.float32,
    )
    poly = COEF_B * gram + COEF_C * square
    product = jnp.einsum(
        "srt,stk->srk",
        poly,
        ortho,
        precision=lax.Precision.HIGHEST,
        preferred_element_type=jnp.float32,
    )
    return COEF_A * ortho + product


def on_device(partials, owner, momentum, master):
    group_count = lax.axis_size("dp")
    local_rows = partials[0]
    block_count = local_rows.shape[0]
    slot_count = momentum.shape[1]
    block_rows = momentum.shape[2]
    owner_list = owner[:, 0]
    target = slot_targets(owner_list, group_count, slot_count)
    present, source = slot_sources(target, group_count * slot_count, block_count)
    outgoing = jnp.where(
        present[:, None, None], jnp.take(local_rows, source, axis=0).astype(jnp.float32), 0.0
    )
    gradient = lax.psum_scatter(outgoing, "dp", scatter_dimension=0, tiled=True)
    momentum_new = BETA * momentum[0] + gradient
    update = gradient + BETA * momentum_new
    squares = lax.psum(jnp.sum(update * update, axis=(1, 2)), "own")
    factor = 1.0 / (jnp.sqrt(squares) + EPSILON)
    ortho = update * factor[:, None, None]
    gram = gram_total(ortho)
    for iteration in range(ITERS):
        if iteration > 0:
            gram = gram_total(ortho)
        ortho = newton_turn(ortho, gram)
    step_factor = STEP_SIZE * 0.2 * math.sqrt(max(block_rows, D))
    master_new = master[0] * (1.0 - STEP_SIZE * DECAY) - step_factor * ortho
    weights_low = master_new.astype(jnp.bfloat16)
    every_slot = lax.all_gather(weights_low, "dp", axis=0, tiled=True)
    weights = jnp.take(every_slot, target, axis=0)
    return (momentum_new[None], master_new[None], weights)


def solution(mesh):
    in_specs = (
        P("dp", None, None, "own"),
        P(),
        P("dp", None, None, "own"),
        P("dp", None, None, "own"),
    )
    out_specs = (P("dp", None, None, "own"), P("dp", None, None, "own"), P(None, None, "own"))
    return jax.shard_map(
        on_device, mesh=mesh, in_specs=in_specs, out_specs=out_specs, check_vma=False
    )
```

profile of v0, /device:TPU:1, one launch (start us, length us, event | category | flops | bytes accessed | tf_op | source)
XLA Modules:
  0.0 780.1 jit_solution(16891098648073873890)
XLA Ops:
  9.8 8.6 %gather_fusion = bf16[128,256,128]{2,1,0:T(8,128)(2,1)} fusion(bf16[64,256,128]{2,1,0:T(8,128)(2,1)} %bitcast.64, s32[1024]{0:T(1024)S(1)} %pad_clamp_fusion.1), kind=kCustom, calls=%fused_computation | custom fusion | bytes 16777728 | tf_op jit(solution)/shard_map/jit(_take)/gather | solution.py:80
  18.4 13.4 %convert_select_fusion = f32[128,256,128]{2,1,0:T(8,128)} fusion(bf16[128,256,128]{2,1,0:T(8,128)(2,1)} %gather_fusion, pred[128]{0:T(512)(128)(4,1)S(1)} %compare_and_fusion, pred[128]{0:T(512)(128)(4,1)S(1)} %fusion.14), kind=kLoop, calls=%fused_computation.2 | loop fusion | flops 12582912 | bytes 25166080 | tf_op jit(solution)/shard_map/jit(_where)/select_n | solution.py:79
  31.8 245.8 %reduce-scatter.2.cloned.1.call-done = f32[4,256,128]{2,1,0:T(8,128)} async-done(((f32[128,256,128]{2,1,0:T(8,128)}), f32[4,256,128]{2,1,0:T(8,128)}) %reduce-scatter.2.cloned.1.call-update) | async-done | bytes 524304 | tf_op jit(solution)/shard_map/reduce_scatter | solution.py:82
  279.6 17.0 %psum.42 = f32[4]{0:T(128)S(1)} all-reduce(f32[4]{0:T(128)S(1)} %get-tuple-element.5), channel_id=1, replica_groups=mesh['dp'=32,'own'=8] {'own'}, use_global_device_ids=true, to_apply=%region_6.7 | all-reduce | flops 4 | bytes 32 | tf_op jit(solution)/shard_map/psum | solution.py:85
  296.6 3.3 fusion.7
  300.0 61.9 %all-reduce.6.cloned.1.call-done = f32[4,256,256]{2,1,0:T(8,128)} async-done(((f32[4,256,256]{2,1,0:T(8,128)}), f32[4,256,256]{2,1,0:T(8,128)}) %all-reduce.6.cloned.1.call-update) | async-done | bytes 1048592 | tf_op jit(solution)/shard_map/psum | solution.py:48
  361.9 3.3 fusion.4
  365.2 2.4 convolution_add_fusion.4
  367.6 2.0 fusion.17
  369.8 67.1 %all-reduce.8.cloned.1.call-done = f32[4,256,256]{2,1,0:T(8,128)} async-done(((f32[4,256,256]{2,1,0:T(8,128)}), f32[4,256,256]{2,1,0:T(8,128)}) %all-reduce.8.cloned.1.call-update) | async-done | bytes 1048592 | tf_op jit(solution)/shard_map/psum | solution.py:48
  436.9 3.3 fusion.3
  441.3 2.0 fusion.18
  443.4 67.3 %all-reduce.10.cloned.1.call-done = f32[4,256,256]{2,1,0:T(8,128)} async-done(((f32[4,256,256]{2,1,0:T(8,128)}), f32[4,256,256]{2,1,0:T(8,128)}) %all-reduce.10.cloned.1.call-update) | async-done | bytes 1048592 | tf_op jit(solution)/shard_map/psum | solution.py:48
  510.7 3.3 fusion.2
  515.1 2.0 fusion.19
  517.1 67.3 %all-reduce.12.cloned.1.call-done = f32[4,256,256]{2,1,0:T(8,128)} async-done(((f32[4,256,256]{2,1,0:T(8,128)}), f32[4,256,256]{2,1,0:T(8,128)}) %all-reduce.12.cloned.1.call-update) | async-done | bytes 1048592 | tf_op jit(solution)/shard_map/psum | solution.py:48
  584.5 3.3 fusion.1
  588.8 2.0 fusion.20
  591.1 67.1 %all-reduce.14.cloned.1.call-done = f32[4,256,256]{2,1,0:T(8,128)} async-done(((f32[4,256,256]{2,1,0:T(8,128)}), f32[4,256,256]{2,1,0:T(8,128)}) %all-reduce.14.cloned.1.call-update) | async-done | bytes 1048592 | tf_op jit(solution)/shard_map/psum | solution.py:48
  658.2 3.3 fusion
  661.5 2.0 fusion.16
  663.6 98.5 %all-gather.2.cloned.1.call-done = bf16[128,256,128]{2,1,0:T(8,128)(2,1)} async-done(((bf16[4,256,128]{2,1,0:T(8,128)(2,1)}), bf16[128,256,128]{2,1,0:T(8,128)(2,1)}) %all-gather.2.cloned.1.call-update) | async-done | bytes 8388624 | tf_op jit(solution)/shard_map/all_gather | solution.py:96
  762.1 6.5 gather_fusion.1
  768.6 4.6 broadcast_select_fusion
  (36 shorter events, 8.5 us)
Async XLA Ops:
  7.2 270.5 %reduce-scatter.2.cloned.1.call-start = ((), (), s32[]{:S(2)}) async-start(), calls=%async_computation.1 | async-start | bytes 17301504 | tf_op jit(solution)/shard_map/reduce_scatter | solution.py:82
  31.7 245.9 %copy-start = (f32[1,4,256,128]{3,2,1,0:T(8,128)S(1)}, f32[1,4,256,128]{3,2,1,0:T(8,128)}, u32[]{:S(2)}) copy-start(f32[1,4,256,128]{3,2,1,0:T(8,128)} %param.6) | copy-start | bytes 1572868
  31.8 330.1 %all-reduce.6.cloned.1.call-start = ((), (), s32[]{:S(2)}) async-start(), calls=%async_computation.2 | async-start | bytes 2097152 | tf_op jit(solution)/shard_map/psum | solution.py:48
  299.9 137.0 %all-reduce.8.cloned.1.call-start = ((), (), s32[]{:S(2)}) async-start(), calls=%async_computation.3 | async-start | bytes 2097152 | tf_op jit(solution)/shard_map/psum | solution.py:48
  369.6 141.1 %all-reduce.10.cloned.1.call-start = ((), (), s32[]{:S(2)}) async-start(), calls=%async_computation.4 | async-start | bytes 2097152 | tf_op jit(solution)/shard_map/psum | solution.py:48
  443.3 141.2 %all-reduce.12.cloned.1.call-start = ((), (), s32[]{:S(2)}) async-start(), calls=%async_computation.5 | async-start | bytes 2097152 | tf_op jit(solution)/shard_map/psum | solution.py:48
  514.0 147.5 %copy-start.1 = (f32[1,4,256,128]{3,2,1,0:T(8,128)S(1)}, f32[1,4,256,128]{3,2,1,0:T(8,128)}, u32[]{:S(2)}) copy-start(f32[1,4,256,128]{3,2,1,0:T(8,128)} %param.7) | copy-start | bytes 1572868
  517.0 146.5 %copy-start.2 = (s32[64,1]{0,1:T(1,128)S(1)}, s32[64,1]{0,1:T(1,128)}, u32[]{:S(2)}) copy-start(s32[64,1]{0,1:T(1,128)} %param.5) | copy-start | bytes 772
  517.1 141.1 %all-reduce.14.cloned.1.call-start = ((), (), s32[]{:S(2)}) async-start(), calls=%async_computation.6 | async-start | bytes 2097152 | tf_op jit(solution)/shard_map/psum | solution.py:48
  590.8 171.3 %all-gather.2.cloned.1.call-start = ((), (), s32[]{:S(2)}) async-start(), calls=%async_computation.7 | async-start | bytes 8650752 | tf_op jit(solution)/shard_map/all_gather | solution.py:96
Sparse Core Ops, SparseCore 0:
  31.9 245.7 reduce-scatter.1
  300.1 61.7 all-reduce.5
  369.7 67.2 all-reduce.7
  443.4 67.2 all-reduce.9
  517.2 67.2 all-reduce.11
  590.9 67.2 all-reduce.13
  663.6 98.4 all-gather.1
where the time goes:
time: 780 us
  waiting for transfers between devices  675 us (87%)
  matrix products  35.2 us (5%)
  other arithmetic  22.5 us (3%)
  blocking collectives  17 us (2%)
  local copies, waits for them, and re-layouts  15.1 us (2%)
  between operations  14.3 us (2%)
    psum x5, waiting for transfers between devices, gram_total(): return lax.psum(local_gram(values), 'own')  331 us
    reduce_scatter x1, waiting for transfers between devices, on_device(): gradient = lax.psum_scatter(outgoing, 'dp', scatter_dimension=0, tiled=True)  246 us
    all_gather x1, waiting for transfers between devices, on_device(): every_slot = lax.all_gather(weights_low, 'dp', axis=0, tiled=True)  98.5 us
    psum x1, blocking collectives, on_device(): squares = lax.psum(jnp.sum(update * update, axis=(1, 2)), 'own')  17 us
    dot_general x5, matrix products, newton_turn(): jnp.einsum('srt,stu->sru', gram, gram, precision=lax.Precision.HIGHEST, p...  16.5 us
  transfers between devices with their start and end apart: 7, of which 7 were waited for; matrix products, arithmetic and copies ran while one was open for 0% of the time, Pallas kernels for 0%

commit v1 on v0

--- a/solution.py
+++ b/solution.py
@@ -13,6 +13,11 @@
 STEP_SIZE = 0.2
 DECAY = 0.1
 EPSILON = 1e-07
+
+
+def summed_here(value, mesh_axis):
+    parts = lax.all_gather(value, mesh_axis)
+    return jnp.sum(parts, axis=0)
 
 
 def slot_targets(owner_list, group_count, slot_count):
@@ -45,7 +50,7 @@
 
 
 def gram_total(values):
-    return lax.psum(local_gram(values), "own")
+    return summed_here(local_gram(values), "own")
 
 
 def newton_turn(ortho, gram):

time: 780 us -> 716 us (0.918)
  waiting for transfers between devices: 675 us -> 601 us
  other arithmetic: 22.5 us -> 42.9 us
  matrix products: 35.2 us -> 23.8 us
    psum x5 -> x0, waiting for transfers between devices: 331 us -> none  [gram_total(): return lax.psum(local_gram(values), 'own')]
    all_gather x0 -> x5, waiting for transfers between devices: none -> 258 us  [summed_here(): parts = lax.all_gather(value, mesh_axis)]
    reduce_sum x0 -> x5, other arithmetic: none -> 20.3 us  [summed_here(): return jnp.sum(parts, axis=0)]
    dot_general x5, matrix products: 16.5 us -> 6.29 us  [newton_turn(): jnp.einsum('srt,stu->sru', gram, gram, precision=lax.Precision.HIGHEST, p...]
where the time goes in v1:
time: 716 us; the launch traced here: 715 us
  waiting for transfers between devices  601 us (84%)
  other arithmetic  42.9 us (6%)
  matrix products  23.8 us (3%)
  blocking collectives  17 us (2%)
  local copies, waits for them, and re-layouts  15.1 us (2%)
  between operations  14.3 us (2%)
    all_gather x5, waiting for transfers between devices, summed_here(): parts = lax.all_gather(value, mesh_axis)  258 us
    reduce_scatter x1, waiting for transfers between devices, on_device(): gradient = lax.psum_scatter(outgoing, 'dp', scatter_dimension=0, tiled=True)  246 us
    all_gather x1, waiting for transfers between devices, on_device(): every_slot = lax.all_gather(weights_low, 'dp', axis=0, tiled=True)  97 us
    reduce_sum x5, other arithmetic, summed_here(): return jnp.sum(parts, axis=0)  20.3 us
    psum x1, blocking collectives, on_device(): squares = lax.psum(jnp.sum(update * update, axis=(1, 2)), 'own')  17 us
  transfers between devices with their start and end apart: 7, of which 7 were waited for; matrix products, arithmetic and copies ran while one was open for 0% of the time, Pallas kernels for 0%

profile of v1, /device:TPU:1, one launch (start us, length us, event | category | flops | bytes accessed | tf_op | source)
XLA Modules:
  0.0 715.1 jit_solution(15275610720060932895)
XLA Ops:
  9.8 8.6 %gather_fusion = bf16[128,256,128]{2,1,0:T(8,128)(2,1)} fusion(bf16[64,256,128]{2,1,0:T(8,128)(2,1)} %bitcast.69, s32[1024]{0:T(1024)S(1)} %pad_clamp_fusion.1), kind=kCustom, calls=%fused_computation | custom fusion | bytes 16777728 | tf_op jit(solution)/shard_map/jit(_take)/gather | solution.py:85
  18.4 13.4 %convert_select_fusion = f32[128,256,128]{2,1,0:T(8,128)} fusion(bf16[128,256,128]{2,1,0:T(8,128)(2,1)} %gather_fusion, pred[128]{0:T(512)(128)(4,1)S(1)} %compare_and_fusion, pred[128]{0:T(512)(128)(4,1)S(1)} %fusion.14), kind=kLoop, calls=%fused_computation.2 | loop fusion | flops 12582912 | bytes 25166080 | tf_op jit(solution)/shard_map/jit(_where)/select_n | solution.py:84
  31.8 245.8 %reduce-scatter.2.cloned.1.call-done = f32[4,256,128]{2,1,0:T(8,128)} async-done(((f32[128,256,128]{2,1,0:T(8,128)}), f32[4,256,128]{2,1,0:T(8,128)}) %reduce-scatter.2.cloned.1.call-update) | async-done | bytes 524304 | tf_op jit(solution)/shard_map/reduce_scatter | solution.py:87
  277.7 2.0 multiply_reduce_fusion
  279.7 17.0 %psum.7 = f32[4]{0:T(128)S(1)} all-reduce(f32[4]{0:T(128)S(1)} %get-tuple-element.5), channel_id=1, replica_groups=mesh['dp'=32,'own'=8] {'own'}, use_global_device_ids=true, to_apply=%region_6.7 | all-reduce | flops 4 | bytes 32 | tf_op jit(solution)/shard_map/psum | solution.py:90
  296.7 3.3 fusion.7
  300.2 48.6 %all-gather.14.cloned.1.call-done = f32[32,256,256]{2,1,0:T(8,128)} async-done(((f32[4,256,256]{2,1,0:T(8,128)}), f32[32,256,256]{2,1,0:T(8,128)}) %all-gather.14.cloned.1.call-update) | async-done | bytes 8388624 | tf_op jit(solution)/shard_map/all_gather | solution.py:19
  348.8 4.1 reduce_sum.80
  355.3 2.0 fusion.17
  357.4 52.5 %all-gather.16.cloned.1.call-done = f32[32,256,256]{2,1,0:T(8,128)} async-done(((f32[4,256,256]{2,1,0:T(8,128)}), f32[32,256,256]{2,1,0:T(8,128)}) %all-gather.16.cloned.1.call-update) | async-done | bytes 8388624 | tf_op jit(solution)/shard_map/all_gather | solution.py:19
  409.9 4.1 reduce_sum.81
  416.3 2.0 fusion.18
  418.6 52.3 %all-gather.18.cloned.1.call-done = f32[32,256,256]{2,1,0:T(8,128)} async-done(((f32[4,256,256]{2,1,0:T(8,128)}), f32[32,256,256]{2,1,0:T(8,128)}) %all-gather.18.cloned.1.call-update) | async-done | bytes 8388624 | tf_op jit(solution)/shard_map/all_gather | solution.py:19
  470.9 4.1 reduce_sum.82
  477.3 2.0 fusion.19
  479.3 52.5 %all-gather.20.cloned.1.call-done = f32[32,256,256]{2,1,0:T(8,128)} async-done(((f32[4,256,256]{2,1,0:T(8,128)}), f32[32,256,256]{2,1,0:T(8,128)}) %all-gather.20.cloned.1.call-update) | async-done | bytes 8388624 | tf_op jit(solution)/shard_map/all_gather | solution.py:19
  531.8 4.1 reduce_sum.83
  538.2 2.0 fusion.20
  540.6 52.3 %all-gather.22.cloned.1.call-done = f32[32,256,256]{2,1,0:T(8,128)} async-done(((f32[4,256,256]{2,1,0:T(8,128)}), f32[32,256,256]{2,1,0:T(8,128)}) %all-gather.22.cloned.1.call-update) | async-done | bytes 8388624 | tf_op jit(solution)/shard_map/all_gather | solution.py:19
  592.8 4.1 reduce_sum.84
  598.2 2.0 fusion.16
  600.2 97.0 %all-gather.12.cloned.1.call-done = bf16[128,256,128]{2,1,0:T(8,128)(2,1)} async-done(((bf16[4,256,128]{2,1,0:T(8,128)(2,1)}), bf16[128,256,128]{2,1,0:T(8,128)(2,1)}) %all-gather.12.cloned.1.call-update) | async-done | bytes 8388624 | tf_op jit(solution)/shard_map/all_gather | solution.py:101
  697.2 6.5 gather_fusion.1
  703.6 4.6 broadcast_select_fusion
  (43 shorter events, 14.3 us)
Async XLA Ops:
  7.2 270.5 %reduce-scatter.2.cloned.1.call-start = ((), (), s32[]{:S(2)}) async-start(), calls=%async_computation.1 | async-start | bytes 17301504 | tf_op jit(solution)/shard_map/reduce_scatter | solution.py:87
  31.7 245.9 %copy-start = (f32[1,4,256,128]{3,2,1,0:T(8,128)S(1)}, f32[1,4,256,128]{3,2,1,0:T(8,128)}, u32[]{:S(2)}) copy-start(f32[1,4,256,128]{3,2,1,0:T(8,128)} %param.6) | copy-start | bytes 1572868
  31.8 317.1 %all-gather.14.cloned.1.call-start = ((), (), s32[]{:S(2)}) async-start(), calls=%async_computation.3 | async-start | bytes 9437184 | tf_op jit(solution)/shard_map/all_gather | solution.py:19
  277.7 76.5 %copy-start.1 = (f32[4,256,128]{2,1,0:T(8,128)S(1)}, f32[4,256,128]{2,1,0:T(8,128)}, u32[]{:S(2)}) copy-start(f32[4,256,128]{2,1,0:T(8,128)} %reduce-scatter.2.cloned.1.call-done) | copy-start | bytes 1572868
  300.0 109.9 %all-gather.16.cloned.1.call-start = ((), (), s32[]{:S(2)}) async-start(), calls=%async_computation.4 | async-start | bytes 9437184 | tf_op jit(solution)/shard_map/all_gather | solution.py:19
  357.3 113.5 %all-gather.18.cloned.1.call-start = ((), (), s32[]{:S(2)}) async-start(), calls=%async_computation.5 | async-start | bytes 9437184 | tf_op jit(solution)/shard_map/all_gather | solution.py:19
  418.3 113.5 %all-gather.20.cloned.1.call-start = ((), (), s32[]{:S(2)}) async-start(), calls=%async_computation.6 | async-start | bytes 9437184 | tf_op jit(solution)/shard_map/all_gather | solution.py:19
  479.3 113.6 %all-gather.22.cloned.1.call-start = ((), (), s32[]{:S(2)}) async-start(), calls=%async_computation.7 | async-start | bytes 9437184 | tf_op jit(solution)/shard_map/all_gather | solution.py:19
  538.2 59.9 %copy-start.2 = (f32[1,4,256,128]{3,2,1,0:T(8,128)S(1)}, f32[1,4,256,128]{3,2,1,0:T(8,128)}, u32[]{:S(2)}) copy-start(f32[1,4,256,128]{3,2,1,0:T(8,128)} %param.7) | copy-start | bytes 1572868
  540.2 59.9 %copy-start.3 = (s32[64,1]{0,1:T(1,128)S(1)}, s32[64,1]{0,1:T(1,128)}, u32[]{:S(2)}) copy-start(s32[64,1]{0,1:T(1,128)} %param.5) | copy-start | bytes 772
  540.2 156.9 %all-gather.12.cloned.1.call-start = ((), (), s32[]{:S(2)}) async-start(), calls=%async_computation.2 | async-start | bytes 8650752 | tf_op jit(solution)/shard_map/all_gather | solution.py:101
Sparse Core Ops, SparseCore 0:
  31.9 245.7 reduce-scatter.1
  300.1 48.6 all-gather.13
  357.4 52.4 all-gather.15
  418.4 52.4 all-gather.17
  479.4 52.4 all-gather.19
  540.4 52.4 all-gather.21
  600.3 96.8 all-gather.11
